TPU v7x, 128 devices: a whole 4x4x4 slice. The times are simulated.
128 devices in a mesh: dp: 4 (over x), expert: 32 (over y, z, core).
Axes of the slice: x: 4, y: 4, z: 4, core: 2. Of those that a mesh axis runs over, the one named last changes fastest.
Arguments:
- tokens: bfloat16 [16384, 4096], P(('dp', 'expert')), may hold values from -6 to 6
- cotangent: bfloat16 [16384, 4096], P(('dp', 'expert')), may hold values from -6 to 6
- routes: int32 [16384], P(('dp', 'expert')), may hold values from 0 to 31, as said below
- combine: float32 [16384], P(('dp', 'expert')), may hold values from 0.05 to 1
- expert_weights: bfloat16 [32, 3, 1536, 4096], P('expert', None, 'dp'), may hold values from -0.09375 to 0.09375
Outputs:
- combined: bfloat16 [16384, 4096], P(('dp', 'expert'))
- token_grad: bfloat16 [16384, 4096], P(('dp', 'expert'))
- combine_grad: float32 [16384], P(('dp', 'expert'))
Inputs may be any that keep to these rules, and one draw needn't show every extreme that they name: `routes`: among the 128 rows of every device, two experts, the same two on every device, are each named by exactly 8 rows, and every other expert by 3 or 4 rows.
All inputs are finite; a program needn't handle non-finite values.
Results may differ from a plain program's by a relative error of at most 0.015.
Values may be sent and summed in bfloat16 or wider, within the bound.
No kernel may reach another device: no remote copies, remote signals or barrier semaphores. Data moves between devices by JAX's collectives and lax.ppermute only.
A program may use at most 192 MiB of HBM per device.

v0:
```python
import jax
import jax.numpy as jnp
from jax import lax
from jax.sharding import PartitionSpec as P


def placement(member, slot_count):
    within = jnp.sum((jnp.cumsum(member, 0) - 1) * member, 1)
    owner_group = jnp.sum(member * lax.iota(jnp.int32, member.shape[1])[None, :], 1)
    is_used = jnp.sum(member, 1) > 0
    target = owner_group * slot_count + within
    buffer_cells = lax.iota(jnp.int32, member.shape[1] * slot_count)
    return ((buffer_cells[:, None] == target[None, :]) & is_used[None, :]).astype(jnp.bfloat16)


def spread(layout, row_block):
    return jnp.dot(layout, row_block, preferred_element_type=jnp.float32).astype(jnp.bfloat16)


def collect(layout, buffer_rows):
    return lax.dot_general(
        layout, buffer_rows, (((0,), (0,)), ((), ())), preferred_element_type=jnp.float32
    )


def group_rows(values):
    return lax.all_gather(values, "dp", axis=0, tiled=True)


def group_sum(values):
    return lax.psum_scatter(
        values.astype(jnp.bfloat16), "dp", scatter_dimension=0, tiled=True
    ).astype(jnp.float32)


def send_rows(cold_buf, experts, slot_count, model_width):
    arrived = lax.all_to_all(
        cold_buf.reshape(experts, slot_count, model_width),
        "expert",
        split_axis=0,
        concat_axis=0,
        tiled=True,
    ).reshape(-1, model_width)
    cold_in = group_rows(arrived)
    hot_in = None
    return (cold_in, hot_in)


def return_rows(cold_part, experts, slot_count, model_width):
    cold_total = group_sum(cold_part)
    hot_out = None
    summed = cold_total.astype(jnp.bfloat16).reshape(experts, slot_count, model_width)
    cold_out = lax.all_to_all(summed, "expert", split_axis=0, concat_axis=0, tiled=True).reshape(
        -1, model_width
    )
    return (cold_out, hot_out)


def forward_rows(row_block, matrices):
    gate_up = jnp.einsum("rd,kfd->krf", row_block, matrices[:2], preferred_element_type=jnp.float32)
    gate_act = gate_up[0]
    up_act = gate_up[1]
    hidden = (gate_act * jax.nn.sigmoid(gate_act) * up_act).astype(jnp.bfloat16)
    partial_out = jnp.dot(hidden, matrices[2], preferred_element_type=jnp.float32)
    return (gate_act, up_act, partial_out)


def backward_rows(row_block, gate_act, up_act, matrices):
    hidden_grad = lax.dot_general(
        row_block, matrices[2], (((1,), (1,)), ((), ())), preferred_element_type=jnp.float32
    )
    squashed = jax.nn.sigmoid(gate_act)
    gate_grad = (hidden_grad * up_act * squashed * (1.0 + gate_act * (1.0 - squashed))).astype(
        jnp.bfloat16
    )
    up_grad = (hidden_grad * gate_act * squashed).astype(jnp.bfloat16)
    both_grads = jnp.stack([gate_grad, up_grad])
    return jnp.einsum("krf,kfd->rd", both_grads, matrices[:2], preferred_element_type=jnp.float32)


def shards(tokens, cotangent, routes, combine, expert_weights):
    weights = expert_weights[0]
    tok_dev = tokens.shape[0]
    model_width = tokens.shape[1]
    experts = lax.axis_size("expert")
    capacity = 2 * tok_dev // experts
    labels = lax.iota(jnp.int32, experts)
    member = (routes[:, None] == labels[None, :]).astype(jnp.int32)
    cold_layout = placement(member, capacity)
    cold_buf = spread(cold_layout, tokens)
    cold_in, hot_in = send_rows(cold_buf, experts, capacity, model_width)
    gate_act, up_act, cold_part = forward_rows(cold_in, weights)
    cold_out, hot_out = return_rows(cold_part, experts, capacity, model_width)
    expert_out = collect(cold_layout, cold_out)
    cotangent_wide = cotangent.astype(jnp.float32)
    combined = (combine[:, None] * expert_out).astype(jnp.bfloat16)
    combine_grad = jnp.sum(expert_out * cotangent_wide, 1)
    out_grad = (combine[:, None] * cotangent_wide).astype(jnp.bfloat16)
    cold_grad_buf = spread(cold_layout, out_grad)
    cold_grad_in, hot_grad_in = send_rows(cold_grad_buf, experts, capacity, model_width)
    cold_grad_part = backward_rows(cold_grad_in, gate_act, up_act, weights)
    cold_grad_out, hot_grad_out = return_rows(cold_grad_part, experts, capacity, model_width)
    input_grad = collect(cold_layout, cold_grad_out)
    token_grad = input_grad.astype(jnp.bfloat16)
    return (combined, token_grad, combine_grad)


def solution(mesh):
    return jax.shard_map(
        shards,
        mesh=mesh,
        in_specs=(
            P(("dp", "expert"), None),
            P(("dp", "expert"), None),
            P(("dp", "expert")),
            P(("dp", "expert")),
            P("expert", None, "dp", None),
        ),
        out_specs=(P(("dp", "expert"), None), P(("dp", "expert"), None), P(("dp", "expert"))),
        check_vma=False,
    )
```

profile of v0, /device:TPU:1, one launch (start us, length us, event | category | flops | bytes accessed | tf_op | source)
XLA Modules:
  0.0 446.6 jit_solution(15779998642776179402)
XLA Ops:
  7.2 0.0 copy-start
  7.2 0.0 all-gather.3.cloned.1.call-start
  7.2 0.8 fusion.49
  8.1 0.2 reduce_window_sum.11
  8.2 0.9 fusion.54
  9.1 0.0 copy-done
  9.1 0.7 fusion.6
  9.8 37.7 %all_to_all.20 = bf16[32,8,4096]{2,1,0:T(8,128)(2,1)} all-to-all(bf16[32,8,4096]{2,1,0:T(8,128)(2,1)S(1)} %fusion.6), channel_id=1, replica_groups=mesh['dp'=4,'expert'=32] {'expert'}, dimensions={0} | all-to-all | bytes 4194304 | tf_op jit(solution)/shard_map/all_to_all | solution.py:37
  47.5 0.0 copy-start.2
  47.5 0.0 copy-start.3
  47.5 0.0 all-gather.3.cloned.1.call-update
  47.5 0.0 all-gather.5.cloned.1.call-start
  47.6 1.1 copy-done.2
  48.7 0.0 copy-done.3
  48.7 0.8 fusion.7
  49.5 32.0 %all_to_all.21 = bf16[32,8,4096]{2,1,0:T(8,128)(2,1)} all-to-all(bf16[32,8,4096]{2,1,0:T(8,128)(2,1)S(1)} %fusion.7), channel_id=1, replica_groups=mesh['dp'=4,'expert'=32] {'expert'}, dimensions={0} | all-to-all | bytes 4194304 | tf_op jit(solution)/shard_map/all_to_all | solution.py:37
  81.5 0.0 all-gather.5.cloned.1.call-update
  81.5 0.0 reduce-scatter.5.cloned.1.call-start
  81.6 46.7 %all-gather.3.cloned.1.call-done = bf16[1024,4096]{1,0:T(8,128)(2,1)} async-done(((bf16[256,4096]{1,0:T(8,128)(2,1)}), bf16[1024,4096]{1,0:T(8,128)(2,1)}) %all-gather.3.cloned.1.call-update) | async-done | bytes 8388624 | tf_op jit(solution)/shard_map/all_gather | solution.py:27
  128.3 12.1 %fusion.18 = f32[2,1024,384]{2,1,0:T(8,128)} fusion(bf16[1,3,384,4096]{3,2,1,0:T(8,128)(2,1)} %param.9, bf16[1024,4096]{1,0:T(8,128)(2,1)} %all-gather.3.cloned.1.call-done), kind=kOutput, calls=%fused_computation.26 | convolution fusion | flops 6442450944 | bytes 17825792 | tf_op jit(solution)/shard_map/rd,kfd->krf/dot_general | solution.py:60
  140.5 73.6 %all-gather.5.cloned.1.call-done = bf16[1024,4096]{1,0:T(8,128)(2,1)} async-done(((bf16[256,4096]{1,0:T(8,128)(2,1)}), bf16[1024,4096]{1,0:T(8,128)(2,1)}) %all-gather.5.cloned.1.call-update) | async-done | bytes 8388624 | tf_op jit(solution)/shard_map/all_gather | solution.py:27
  214.1 10.1 %fusion.39 = (bf16[1,1024,384]{2,1,0:T(8,128)(2,1)S(1)}, bf16[1,1024,384]{2,1,0:T(8,128)(2,1)S(1)}) fusion(f32[2,1024,384]{2,1,0:T(8,128)} %fusion.18, bf16[1024,4096]{1,0:T(8,128)(2,1)} %all-gather.5.cloned.1.call-done, bf16[1,3,384,4096]{3,2,1,0:T(8,128)(2,1)} %param.9), kind=kOutput, calls=%fused_computation.47 | convolution fusion | flops 3226337280 | bytes 16252928 | tf_op jit(solution)/shard_map/dot_general | solution.py:69
  224.2 11.5 %bitcast_convert_fusion = bf16[1024,4096]{1,0:T(8,128)(2,1)} fusion(bf16[1,3,384,4096]{3,2,1,0:T(8,128)(2,1)} %param.9, bf16[1,1024,384]{2,1,0:T(8,128)(2,1)S(1)} %get-tuple-element.7, bf16[1,1024,384]{2,1,0:T(8,128)(2,1)S(1)} %get-tuple-element.6), kind=kOutput, calls=%fused_computation | convolution fusion | flops 6447431680 | bytes 16252928 | tf_op jit(solution)/shard_map/krf,kfd->rd/dot_general | solution.py:78
  235.7 0.0 reduce-scatter.5.cloned.1.call-update
  235.7 0.2 reduce-scatter.3.cloned.1.call-start
  235.9 11.0 %convolution_convert_fusion = bf16[1024,4096]{1,0:T(8,128)(2,1)} fusion(bf16[1,3,384,4096]{3,2,1,0:T(8,128)(2,1)} %param.9, f32[2,1024,384]{2,1,0:T(8,128)} %fusion.18), kind=kOutput, calls=%fused_computation.3 | convolution fusion | flops 3227779072 | bytes 14680064 | tf_op jit(solution)/shard_map/dot_general | solution.py:64
  246.9 0.0 reduce-scatter.3.cloned.1.call-update
  246.9 70.4 %reduce-scatter.5.cloned.1.call-done = bf16[256,4096]{1,0:T(8,128)(2,1)} async-done(((bf16[1024,4096]{1,0:T(8,128)(2,1)}), bf16[256,4096]{1,0:T(8,128)(2,1)}) %reduce-scatter.5.cloned.1.call-update) | async-done | bytes 2097168 | tf_op jit(solution)/shard_map/reduce_scatter | solution.py:31
  317.4 7.6 %all-to-all-start.3 = ((bf16[32,8,4096]{2,1,0:T(8,128)(2,1)}), bf16[32,8,4096]{2,1,0:T(8,128)(2,1)S(1)}, u32[]{:S(2)}, u32[]{:S(2)}) async-start(bf16[32,8,4096]{2,1,0:T(8,128)(2,1)} %bitcast.86), calls=%async_computation.5 | async-start | bytes 4194304 | tf_op jit(solution)/shard_map/all_to_all | solution.py:53
  325.0 74.9 %reduce-scatter.3.cloned.1.call-done = bf16[256,4096]{1,0:T(8,128)(2,1)} async-done(((bf16[1024,4096]{1,0:T(8,128)(2,1)}), bf16[256,4096]{1,0:T(8,128)(2,1)}) %reduce-scatter.3.cloned.1.call-update) | async-done | bytes 2097168 | tf_op jit(solution)/shard_map/reduce_scatter | solution.py:31
  399.9 0.0 all-to-all-done.3
  399.9 7.7 %all-to-all-start.1 = ((bf16[32,8,4096]{2,1,0:T(8,128)(2,1)}), bf16[32,8,4096]{2,1,0:T(8,128)(2,1)}, u32[]{:S(2)}, u32[]{:S(2)}) async-start(bf16[32,8,4096]{2,1,0:T(8,128)(2,1)} %bitcast.87), calls=%async_computation.2 | async-start | bytes 4194304 | tf_op jit(solution)/shard_map/all_to_all | solution.py:53
  407.6 0.0 copy-start.1
  407.6 1.5 convolution_convert_fusion.3
  409.1 26.9 %all-to-all-done.1 = bf16[32,8,4096]{2,1,0:T(8,128)(2,1)} async-done(((bf16[32,8,4096]{2,1,0:T(8,128)(2,1)}), bf16[32,8,4096]{2,1,0:T(8,128)(2,1)}, u32[]{:S(2)}, u32[]{:S(2)}) %all-to-all-start.1) | async-done | bytes 2097184 | tf_op jit(solution)/shard_map/all_to_all | solution.py:53
  436.0 4.1 fusion.14
  440.1 0.0 copy-done.1
  (2 shorter events, 0.0 us)
Async XLA Ops:
  7.2 2.0 copy-start
  7.2 121.1 %all-gather.3.cloned.1.call-start = ((), (), s32[]{:S(2)}) async-start(), calls=%async_computation.6 | async-start | bytes 10485760 | tf_op jit(solution)/shard_map/all_gather | solution.py:27
  47.5 1.2 copy-start.2
  47.5 1.2 copy-start.3
  47.5 166.6 %all-gather.5.cloned.1.call-start = ((), (), s32[]{:S(2)}) async-start(), calls=%async_computation.8 | async-start | bytes 10485760 | tf_op jit(solution)/shard_map/all_gather | solution.py:27
  81.5 235.8 %reduce-scatter.5.cloned.1.call-start = ((), (), s32[]{:S(2)}) async-start(), calls=%async_computation.9 | async-start | bytes 10485760 | tf_op jit(solution)/shard_map/reduce_scatter | solution.py:31
  235.7 164.2 %reduce-scatter.3.cloned.1.call-start = ((), (), s32[]{:S(2)}) async-start(), calls=%async_computation.7 | async-start | bytes 10485760 | tf_op jit(solution)/shard_map/reduce_scatter | solution.py:31
  317.4 82.6 %all-to-all-start.3 = ((bf16[32,8,4096]{2,1,0:T(8,128)(2,1)}), bf16[32,8,4096]{2,1,0:T(8,128)(2,1)S(1)}, u32[]{:S(2)}, u32[]{:S(2)}) async-start(bf16[32,8,4096]{2,1,0:T(8,128)(2,1)} %bitcast.86), calls=%async_computation.5 | async-start | bytes 4194304 | tf_op jit(solution)/shard_map/all_to_all | solution.py:53
  399.9 36.1 %all-to-all-start.1 = ((bf16[32,8,4096]{2,1,0:T(8,128)(2,1)}), bf16[32,8,4096]{2,1,0:T(8,128)(2,1)}, u32[]{:S(2)}, u32[]{:S(2)}) async-start(bf16[32,8,4096]{2,1,0:T(8,128)(2,1)} %bitcast.87), calls=%async_computation.2 | async-start | bytes 4194304 | tf_op jit(solution)/shard_map/all_to_all | solution.py:53
  407.6 32.4 %copy-start.1 = (bf16[128,4096]{1,0:T(8,128)(2,1)S(1)}, bf16[128,4096]{1,0:T(8,128)(2,1)}, u32[]{:S(2)}) copy-start(bf16[128,4096]{1,0:T(8,128)(2,1)} %param.5) | copy-start | bytes 3145732
Sparse Core Ops, SparseCore 0:
  47.6 80.6 all-gather.2
  130.0 84.0 all-gather.4
  235.8 81.4 reduce-scatter.4
  319.7 80.1 reduce-scatter.2
where the time goes:
time: 447 us
  waiting for transfers between devices  293 us (66%)
  blocking collectives  69.7 us (16%)
  matrix products  51.7 us (12%)
  starting transfers between devices  15.7 us (4%)
  between operations  13.9 us (3%)
    reduce_scatter x2, waiting for transfers between devices, group_sum(): lax.psum_scatter(values.astype(jnp.bfloat16), 'dp', scatter_dimension=0,...  145 us
    all_gather x2, waiting for transfers between devices, group_rows(): return lax.all_gather(values, 'dp', axis=0, tiled=True)  120 us
    all_to_all x2, blocking collectives, send_rows(): lax.all_to_all(cold_buf.reshape(experts, slot_count, model_width), 'exper...  69.7 us
    all_to_all x2, waiting for transfers between devices, return_rows(): lax.all_to_all(summed, 'expert', split_axis=0, concat_axis=0, tiled=True)  26.9 us
    all_to_all x2, starting transfers between devices, return_rows(): lax.all_to_all(summed, 'expert', split_axis=0, concat_axis=0, tiled=True)  15.3 us
    dot_general x1, matrix products, forward_rows(): jnp.einsum('rd,kfd->krf', row_block, matrices[:2], preferred_element_type...  12.1 us
    dot_general x1, matrix products, backward_rows(): jnp.einsum('krf,kfd->rd', both_grads, matrices[:2], preferred_element_typ...  11.5 us
    dot_general x1, matrix products, forward_rows(): jnp.dot(hidden, matrices[2], preferred_element_type=jnp.float32)  11 us
  transfers between devices with their start and end apart: 6, of which 5 were waited for; matrix products, arithmetic and copies ran while one was open for 6% of the time, Pallas kernels for 0%

commit v1 on v0

--- a/solution.py
+++ b/solution.py
@@ -24,7 +24,9 @@
 
 
 def group_rows(values):
-    return lax.all_gather(values, "dp", axis=0, tiled=True)
+    return jnp.concatenate(
+        lax.all_to_all(jnp.stack([values] * lax.axis_size("dp")), "dp", 0, 0), axis=0
+    )
 
 
 def group_sum(values):

time: 447 us -> 476 us (1.065)
  blocking collectives: 69.7 us -> 298 us
  waiting for transfers between devices: 293 us -> 97.2 us
  matrix products: 51.7 us -> 43.9 us
    all_to_all x0 -> x2, blocking collectives: none -> 228 us  [group_rows(): lax.all_to_all(jnp.stack([values] * lax.axis_size('dp')), 'dp', 0, 0)]
    all_gather x2 -> x0, waiting for transfers between devices: 120 us -> none  [group_rows(): return lax.all_gather(values, 'dp', axis=0, tiled=True)]
    reduce_scatter x2, waiting for transfers between devices: 145 us -> 72.4 us  [group_sum(): lax.psum_scatter(values.astype(jnp.bfloat16), 'dp', scatter_dimension=0,...]
  transfers between devices with their start and end apart: 6 -> 4, of which waited for: 5 -> 2; matrix products, arithmetic and copies ran while one was open for 6% -> 5% of each run, Pallas kernels for 0% -> 0%
where the time goes in v1:
time: 476 us; the launch traced here: 475 us
  blocking collectives  298 us (63%)
  waiting for transfers between devices  97.2 us (20%)
  matrix products  43.9 us (9%)
  starting transfers between devices  15.4 us (3%)
  between operations  14.2 us (3%)
  local copies, waits for them, and re-layouts  5.01 us (1%)
    all_to_all x2, blocking collectives, group_rows(): lax.all_to_all(jnp.stack([values] * lax.axis_size('dp')), 'dp', 0, 0)  228 us
    reduce_scatter x2, waiting for transfers between devices, group_sum(): lax.psum_scatter(values.astype(jnp.bfloat16), 'dp', scatter_dimension=0,...  72.4 us
    all_to_all x2, blocking collectives, send_rows(): lax.all_to_all(cold_buf.reshape(experts, slot_count, model_width), 'exper...  70.3 us
    all_to_all x2, waiting for transfers between devices, return_rows(): lax.all_to_all(summed, 'expert', split_axis=0, concat_axis=0, tiled=True)  24.7 us
    all_to_all x2, starting transfers between devices, return_rows(): lax.all_to_all(summed, 'expert', split_axis=0, concat_axis=0, tiled=True)  15.3 us
    dot_general x1, matrix products, forward_rows(): jnp.einsum('rd,kfd->krf', row_block, matrices[:2], preferred_element_type...  11 us
  transfers between devices with their start and end apart: 4, of which 2 were waited for; matrix products, arithmetic and copies ran while one was open for 5% of the time, Pallas kernels for 0%

profile of v1, /device:TPU:1, one launch (start us, length us, event | category | flops | bytes accessed | tf_op | source)
XLA Modules:
  0.0 475.4 jit_solution(17632065826538604843)
XLA Ops:
  7.2 0.0 copy-start
  7.2 0.0 reduce-scatter.3.cloned.1.call-start
  7.2 0.8 fusion.46
  8.1 0.2 reduce_window_sum.11
  8.2 0.9 fusion.51
  9.1 0.0 copy-done
  9.1 0.7 fusion.5
  9.8 37.6 %all_to_all.30 = bf16[32,8,4096]{2,1,0:T(8,128)(2,1)S(1)} all-to-all(bf16[32,8,4096]{2,1,0:T(8,128)(2,1)S(1)} %fusion.5), channel_id=1, replica_groups=mesh['dp'=4,'expert'=32] {'expert'}, dimensions={0} | all-to-all | bytes 4194304 | tf_op jit(solution)/shard_map/all_to_all | solution.py:39
  47.4 1.0 stack.15
  48.4 97.2 %all_to_all.31 = bf16[4,256,4096]{2,1,0:T(8,128)(2,1)S(1)} all-to-all(bf16[4,256,4096]{2,1,0:T(8,128)(2,1)S(1)} %stack.15), channel_id=1, replica_groups=mesh['dp'=4,'expert'=32] {'dp'}, dimensions={0} | all-to-all | bytes 16777216 | tf_op jit(solution)/shard_map/all_to_all | solution.py:28
  145.7 11.0 %fusion.17 = f32[2,1024,384]{2,1,0:T(8,128)S(1)} fusion(bf16[1024,4096,1]{1,0,2:T(8,128)(2,1)S(1)} %bitcast.87, bf16[1,3,384,4096]{3,2,1,0:T(8,128)(2,1)} %param.9), kind=kOutput, calls=%fused_computation.25 | convolution fusion | flops 6442450944 | bytes 17825792 | tf_op jit(solution)/shard_map/rd,kfd->krf/dot_general | solution.py:62
  156.6 0.0 copy-start.4
  156.6 1.7 copy-done.4
  158.4 8.6 %convolution_convert_fusion = bf16[1024,4096]{1,0:T(8,128)(2,1)} fusion(bf16[1,3,384,4096]{3,2,1,0:T(8,128)(2,1)} %param.9, f32[2,1024,384]{2,1,0:T(8,128)S(1)} %fusion.17), kind=kOutput, calls=%fused_computation.1 | convolution fusion | flops 3227779072 | bytes 14680064 | tf_op jit(solution)/shard_map/dot_general | solution.py:66
  167.0 0.0 copy-start.2
  167.0 0.0 copy-start.3
  167.0 0.0 reduce-scatter.3.cloned.1.call-update
  167.0 0.0 reduce-scatter.5.cloned.1.call-start
  167.1 1.1 copy-done.2
  168.2 0.0 copy-done.3
  168.2 0.8 fusion.6
  169.0 32.7 %all_to_all.32 = bf16[32,8,4096]{2,1,0:T(8,128)(2,1)S(1)} all-to-all(bf16[32,8,4096]{2,1,0:T(8,128)(2,1)S(1)} %fusion.6), channel_id=1, replica_groups=mesh['dp'=4,'expert'=32] {'expert'}, dimensions={0} | all-to-all | bytes 4194304 | tf_op jit(solution)/shard_map/all_to_all | solution.py:39
  201.7 1.0 stack.16
  202.8 0.0 slice-start
  202.8 130.3 %all_to_all.33 = bf16[4,256,4096]{2,1,0:T(8,128)(2,1)S(1)} all-to-all(bf16[4,256,4096]{2,1,0:T(8,128)(2,1)S(1)} %stack.16), channel_id=1, replica_groups=mesh['dp'=4,'expert'=32] {'dp'}, dimensions={0} | all-to-all | bytes 16777216 | tf_op jit(solution)/shard_map/all_to_all | solution.py:28
  333.1 0.0 slice-start.1
  333.1 0.0 slice-start.2
  333.1 7.5 %fusion.36 = (bf16[1,1024,384]{2,1,0:T(8,128)(2,1)S(1)}, bf16[1,1024,384]{2,1,0:T(8,128)(2,1)S(1)}) fusion(f32[2,1024,384]{2,1,0:T(8,128)} %copy-done.4, bf16[1024,4096]{1,0:T(8,128)(2,1)S(1)} %bitcast.86, bf16[1,3,384,4096]{3,2,1,0:T(8,128)(2,1)} %param.9), kind=kOutput, calls=%fused_computation.46 | convolution fusion | flops 3226337280 | bytes 16252928 | tf_op jit(solution)/shard_map/dot_general | solution.py:71
  340.7 0.0 slice-done
  340.7 0.0 slice-done.1
  340.7 0.0 slice-done.2
  340.7 8.6 %bitcast_convert_fusion = bf16[1024,4096]{1,0:T(8,128)(2,1)} fusion(bf16[1,3,384,4096]{3,2,1,0:T(8,128)(2,1)S(1)} %bitcast.91, bf16[1,1024,384]{2,1,0:T(8,128)(2,1)S(1)} %get-tuple-element.7, bf16[1,1024,384]{2,1,0:T(8,128)(2,1)S(1)} %get-tuple-element.6), kind=kOutput, calls=%fused_computation | convolution fusion | flops 6447431680 | bytes 16252928 | tf_op jit(solution)/shard_map/krf,kfd->rd/dot_general | solution.py:80
  349.3 0.0 reduce-scatter.5.cloned.1.call-update
  349.4 0.0 reduce-scatter.3.cloned.1.call-done
  349.4 7.6 %all-to-all-start.2 = ((bf16[32,8,4096]{2,1,0:T(8,128)(2,1)}), bf16[32,8,4096]{2,1,0:T(8,128)(2,1)S(1)}, u32[]{:S(2)}, u32[]{:S(2)}) async-start(bf16[32,8,4096]{2,1,0:T(8,128)(2,1)} %bitcast.88), calls=%async_computation.3 | async-start | bytes 4194304 | tf_op jit(solution)/shard_map/all_to_all | solution.py:55
  357.0 72.4 %reduce-scatter.5.cloned.1.call-done = bf16[256,4096]{1,0:T(8,128)(2,1)} async-done(((bf16[1024,4096]{1,0:T(8,128)(2,1)}), bf16[256,4096]{1,0:T(8,128)(2,1)}) %reduce-scatter.5.cloned.1.call-update) | async-done | bytes 2097168 | tf_op jit(solution)/shard_map/reduce_scatter | solution.py:33
  429.4 0.0 all-to-all-done.2
  429.4 7.7 %all-to-all-start.5 = ((bf16[32,8,4096]{2,1,0:T(8,128)(2,1)}), bf16[32,8,4096]{2,1,0:T(8,128)(2,1)}, u32[]{:S(2)}, u32[]{:S(2)}) async-start(bf16[32,8,4096]{2,1,0:T(8,128)(2,1)} %bitcast.89), calls=%async_computation.7 | async-start | bytes 4194304 | tf_op jit(solution)/shard_map/all_to_all | solution.py:55
  437.1 0.0 copy-start.1
  437.1 3.6 fusion.13
  440.7 24.7 %all-to-all-done.5 = bf16[32,8,4096]{2,1,0:T(8,128)(2,1)} async-done(((bf16[32,8,4096]{2,1,0:T(8,128)(2,1)}), bf16[32,8,4096]{2,1,0:T(8,128)(2,1)}, u32[]{:S(2)}, u32[]{:S(2)}) %all-to-all-start.5) | async-done | bytes 2097184 | tf_op jit(solution)/shard_map/all_to_all | solution.py:55
  465.5 3.1 convolution_convert_fusion.3
  468.5 0.0 copy-done.1
  (3 shorter events, 0.0 us)
Async XLA Ops:
  7.2 2.0 copy-start
  7.2 342.2 %reduce-scatter.3.cloned.1.call-start = ((), (), s32[]{:S(2)}) async-start(), calls=%async_computation.8 | async-start | bytes 10485760 | tf_op jit(solution)/shard_map/reduce_scatter | solution.py:33
  156.6 1.7 copy-start.4
  167.0 1.2 copy-start.2
  167.0 1.2 copy-start.3
  167.0 262.4 %reduce-scatter.5.cloned.1.call-start = ((), (), s32[]{:S(2)}) async-start(), calls=%async_computation.9 | async-start | bytes 10485760 | tf_op jit(solution)/shard_map/reduce_scatter | solution.py:33
  202.8 137.9 %slice-start = ((s8[9437184]{0:T(1024)(128)(4,1)}), s8[4194304]{0:T(1024)(128)(4,1)S(1)}, s32[]{:S(2)}) async-start(s8[9437184]{0:T(1024)(128)(4,1)} %bitcast.90), calls=%async_computation.10 | async-start | bytes 8388608
  333.1 7.6 %slice-start.1 = ((s8[9437184]{0:T(1024)(128)(4,1)}), s8[4194304]{0:T(1024)(128)(4,1)S(1)}, s32[]{:S(2)}) async-start(s8[9437184]{0:T(1024)(128)(4,1)} %bitcast.90), calls=%async_computation.11 | async-start | bytes 8388608
  333.1 7.6 %slice-start.2 = ((s8[9437184]{0:T(1024)(128)(4,1)}), s8[1048576]{0:T(1024)(128)(4,1)S(1)}, s32[]{:S(2)}) async-start(s8[9437184]{0:T(1024)(128)(4,1)} %bitcast.90), calls=%async_computation.12 | async-start | bytes 2097152
  349.4 80.0 %all-to-all-start.2 = ((bf16[32,8,4096]{2,1,0:T(8,128)(2,1)}), bf16[32,8,4096]{2,1,0:T(8,128)(2,1)S(1)}, u32[]{:S(2)}, u32[]{:S(2)}) async-start(bf16[32,8,4096]{2,1,0:T(8,128)(2,1)} %bitcast.88), calls=%async_computation.3 | async-start | bytes 4194304 | tf_op jit(solution)/shard_map/all_to_all | solution.py:55
  429.4 36.1 %all-to-all-start.5 = ((bf16[32,8,4096]{2,1,0:T(8,128)(2,1)}), bf16[32,8,4096]{2,1,0:T(8,128)(2,1)}, u32[]{:S(2)}, u32[]{:S(2)}) async-start(bf16[32,8,4096]{2,1,0:T(8,128)(2,1)} %bitcast.89), calls=%async_computation.7 | async-start | bytes 4194304 | tf_op jit(solution)/shard_map/all_to_all | solution.py:55
  437.1 31.4 %copy-start.1 = (bf16[128,4096]{1,0:T(8,128)(2,1)S(1)}, bf16[128,4096]{1,0:T(8,128)(2,1)}, u32[]{:S(2)}) copy-start(bf16[128,4096]{1,0:T(8,128)(2,1)} %param.5) | copy-start | bytes 3145732
Sparse Core Ops, SparseCore 0:
  167.1 141.5 reduce-scatter.2
  349.5 79.8 reduce-scatter.4
